TPU v7x, 256 devices: a whole 4x4x8 slice. The times are simulated.
256 devices in a mesh: row: 8 (over z), col: 32 (over y, x, core).
Axes of the slice: x: 4, y: 4, z: 8, core: 2. Of those that a mesh axis runs over, the one named last changes fastest.
Arguments:
- features: bfloat16 [32768, 128], P(('row', 'col')), may hold values from -6 to 6
- first_weight: bfloat16 [128, 512], replicated, may hold values from -0.5 to 0.5
- second_weight: bfloat16 [512, 128], replicated, may hold values from -0.25 to 0.25
- tile_rows: int32 [8, 32, 80], P('row', 'col'), may hold values from 0 to 31
- tile_cols: int32 [8, 32, 80], P('row', 'col'), may hold values from 0 to 7
- tile_live: int32 [8, 32], P('row', 'col'), may hold values from 1 to 80, as said below
- column_mask: int32 [8, 32, 80, 128], P('row', 'col'), may hold values 0 or 1
- edge_weight: bfloat16 [8, 32, 80, 128, 128], P('row', 'col'), may hold values from 0.049804688 to 1
- cotangent: bfloat16 [32768, 128], P(('row', 'col')), may hold values from -6 to 6
Outputs:
- output: bfloat16 [32768, 128], P(('row', 'col'))
- first_grad: float32 [128, 512], replicated
- second_grad: float32 [512, 128], replicated
Inputs may be any that keep to these rules, and one draw needn't show every extreme that they name: `tile_live`: slots at or past a device's count are unused; every device of the last column group of the grid uses all 80.
All inputs are finite; a program needn't handle non-finite values. No bound on the sum of `column_mask` on one device may be relied on, other than what follows from the above.
Results may differ from a plain program's by a relative error of at most 0.014.
Values may be sent and summed in bfloat16 or wider, within the bound.
No kernel may reach another device: no remote copies, remote signals or barrier semaphores. Data moves between devices by JAX's collectives and lax.ppermute only.
A program may use at most 128 MiB of HBM per device.

v0:
```python
import math
import jax
import jax.numpy as jnp
from jax import lax
from jax.sharding import PartitionSpec as P

BLOCK = 128
gelu_coef = math.sqrt(2.0 / math.pi)


def gelu_tanh(value):
    return 0.5 * value * (1.0 + jnp.tanh(gelu_coef * (value + 0.044715 * value * value * value)))


def gelu_slope(value):
    tanh_value = jnp.tanh(gelu_coef * (value + 0.044715 * value * value * value))
    return 0.5 * (1.0 + tanh_value) + 0.5 * value * (1.0 - tanh_value * tanh_value) * gelu_coef * (
        1.0 + 3.0 * 0.044715 * value * value
    )


def slot_batches(tile_values, target_index, source_index):
    slot_count = tile_values.shape[0]
    group_size = 16
    batches = slot_count // group_size
    return (
        tile_values.reshape(batches, group_size, BLOCK, BLOCK),
        target_index.reshape(batches, group_size),
        source_index.reshape(batches, group_size),
    )


def forward_part(tile_values, row_index, col_index, panel, target_blocks):
    feature_width = panel.shape[1]
    source_blocks = panel.reshape(-1, BLOCK, feature_width)

    def forward_accumulate(running, slot_piece):
        values_here, rows_here, cols_here = slot_piece
        contrib = jnp.einsum(
            "sij,sjf->sif",
            values_here,
            source_blocks[cols_here],
            preferred_element_type=jnp.float32,
        )
        return (running.at[rows_here].add(contrib), None)

    start = jnp.zeros((target_blocks, BLOCK, feature_width), jnp.float32)
    running, _ = lax.scan(
        forward_accumulate, start, slot_batches(tile_values, row_index, col_index)
    )
    return running.reshape(-1, feature_width)


def backward_part(tile_values, col_index, row_index, panel, target_blocks):
    feature_width = panel.shape[1]
    source_blocks = panel.reshape(-1, BLOCK, feature_width)

    def backward_accumulate(running, slot_piece):
        values_here, cols_here, rows_here = slot_piece
        contrib = jnp.einsum(
            "sij,sif->sjf",
            values_here,
            source_blocks[rows_here],
            preferred_element_type=jnp.float32,
        )
        return (running.at[cols_here].add(contrib), None)

    start = jnp.zeros((target_blocks, BLOCK, feature_width), jnp.float32)
    running, _ = lax.scan(
        backward_accumulate, start, slot_batches(tile_values, col_index, row_index)
    )
    return running.reshape(-1, feature_width)


def local(
    features,
    first_weight,
    second_weight,
    tile_rows,
    tile_cols,
    tile_live,
    column_mask,
    edge_weight,
    cotangent,
):
    slot_count = edge_weight.shape[2]
    node_count = features.shape[0]
    live_slots = (jnp.arange(slot_count, dtype=jnp.int32) < tile_live[0, 0]).astype(jnp.bfloat16)
    tile_values = (
        edge_weight[0, 0]
        * column_mask[0, 0].astype(jnp.bfloat16)[:, None, :]
        * live_slots[:, None, None]
    )
    row_index = tile_rows[0, 0]
    col_index = tile_cols[0, 0]
    row_groups = lax.axis_size("col") * node_count // BLOCK
    col_groups = lax.axis_size("row") * node_count // BLOCK
    row_sums = jnp.sum(tile_values.astype(jnp.float32), axis=2)
    degree_part = (
        jnp.zeros((row_groups, BLOCK), jnp.float32).at[row_index].add(row_sums).reshape(-1)
    )
    panel_in = lax.all_gather(features, "row", axis=0, tiled=True)
    partial_in = forward_part(tile_values, row_index, col_index, panel_in, row_groups)
    degree = lax.psum_scatter(degree_part, "col", scatter_dimension=0, tiled=True)
    summed_in = lax.psum_scatter(
        partial_in.astype(jnp.bfloat16), "col", scatter_dimension=0, tiled=True
    ).astype(jnp.float32)
    row_scale = (1.0 / jnp.sqrt(1.0 + degree))[:, None]
    first_mix = (features.astype(jnp.float32) + row_scale * summed_in).astype(jnp.bfloat16)
    first_pre = jnp.dot(first_mix, first_weight, preferred_element_type=jnp.float32)
    hidden = gelu_tanh(first_pre).astype(jnp.bfloat16)
    panel_hidden = lax.all_gather(hidden, "row", axis=0, tiled=True)
    partial_hidden = forward_part(tile_values, row_index, col_index, panel_hidden, row_groups)
    summed_hidden = lax.psum_scatter(
        partial_hidden.astype(jnp.bfloat16), "col", scatter_dimension=0, tiled=True
    ).astype(jnp.float32)
    second_mix = (hidden.astype(jnp.float32) + row_scale * summed_hidden).astype(jnp.bfloat16)
    output = jnp.dot(second_mix, second_weight, preferred_element_type=jnp.float32).astype(
        jnp.bfloat16
    )
    mix_grad = jnp.einsum("no,ho->nh", cotangent, second_weight, preferred_element_type=jnp.float32)
    scaled_grad = (row_scale * mix_grad).astype(jnp.bfloat16)
    grad_rows = lax.all_gather(scaled_grad, "col", axis=0, tiled=True)
    returned = lax.psum_scatter(
        backward_part(tile_values, col_index, row_index, grad_rows, col_groups).astype(
            jnp.bfloat16
        ),
        "row",
        scatter_dimension=0,
        tiled=True,
    ).astype(jnp.float32)
    hidden_grad = mix_grad + returned
    second_term = jnp.einsum("nh,no->ho", second_mix, cotangent, preferred_element_type=jnp.float32)
    pre_grad = (hidden_grad * gelu_slope(first_pre)).astype(jnp.bfloat16)
    first_term = jnp.einsum("ni,nh->ih", first_mix, pre_grad, preferred_element_type=jnp.float32)
    node_scale = 1.0 / math.sqrt(node_count * lax.axis_size("row") * lax.axis_size("col"))
    first_grad, second_grad = lax.psum(
        (first_term * node_scale, second_term * node_scale), ("row", "col")
    )
    return (output, first_grad, second_grad)


def solution(mesh):
    return jax.shard_map(
        local,
        mesh=mesh,
        in_specs=(
            P(("row", "col"), None),
            P(),
            P(),
            P("row", "col", None),
            P("row", "col", None),
            P("row", "col"),
            P("row", "col", None, None),
            P("row", "col", None, None, None),
            P(("row", "col"), None),
        ),
        out_specs=(P(("row", "col"), None), P(), P()),
        check_vma=False,
    )
```

profile of v0, /device:TPU:2, one launch (start us, length us, event | category | flops | bytes accessed | tf_op | source)
XLA Modules:
  0.0 728.3 jit_solution(3400894786560194901)
XLA Ops:
  12.0 28.8 %all_gather.9 = bf16[1024,128]{1,0:T(8,128)(2,1)S(1)} all-gather(bf16[128,128]{1,0:T(8,128)(2,1)} %param.15), channel_id=1, replica_groups=mesh['row'=8,'col'=32] {'row'}, dimensions={0}, use_global_device_ids=true | all-gather | bytes 294912 | tf_op jit(solution)/shard_map/all_gather | solution.py:102
  40.8 4.4 copy.15
  45.2 4.0 multiply_multiply_fusion
  49.1 4.4 copy.16
  55.1 26.7 %while.30 = (s32[]{:T(128)}, f32[32,128,128]{2,1,0:T(8,128)}, s32[5,16]{1,0:T(8,128)S(1)}, bf16[5,16,128,128]{3,2,1,0:T(8,128)(2,1)}, s32[5,16]{1,0:T(8,128)S(1)}, /*index=5*/bf16[8,128,128]{2,1,0:T(8,128)(2,1)S(1)}, s32[]{:T(128)}) while((s32[]{:T(128)}, f32[32,128,128]{2,1,0:T(8,128)}, s32[5,16]{1,0:T(8,128)S(1)}, ...), condition=%wide.region_5.6_spmd, body=%wide.region_3.0_spmd.sunk | while | flops 67372128 | bytes 6296093 | solution.py:48
  57.1 3.4 scatter_fusion
  62.5 3.3 scatter_fusion
  67.8 3.3 scatter_fusion
  73.1 3.3 scatter_fusion
  78.5 3.3 scatter_fusion
  81.8 2.9 convert_element_type.85
  86.1 1.8 convert_reduce_fusion
  88.8 119.0 %all-reduce = f32[4096]{0:T(1024)S(1)} all-reduce(f32[4096]{0:T(1024)S(1)} %bitcast.122), channel_id=2, replica_groups=mesh['row'=8,'col'=32] {'col'}, use_global_device_ids=true, to_apply=%region_2.3.clone | all-reduce | flops 4096 | bytes 32768
  210.6 36.8 %all-gather.3.cloned.1.call-done = bf16[1024,512]{1,0:T(8,128)(2,1)} async-done(((bf16[128,512]{1,0:T(8,128)(2,1)}), bf16[1024,512]{1,0:T(8,128)(2,1)}) %all-gather.3.cloned.1.call-update) | async-done | bytes 1048592 | tf_op jit(solution)/shard_map/all_gather | solution.py:112
  247.4 4.3 broadcast_in_dim.12
  251.7 69.8 %while.31 = (s32[]{:T(128)}, f32[32,128,512]{2,1,0:T(8,128)}, s32[5,16]{1,0:T(8,128)S(1)}, bf16[5,16,128,128]{3,2,1,0:T(8,128)(2,1)}, s32[5,16]{1,0:T(8,128)S(1)}, /*index=5*/bf16[8,128,512]{2,1,0:T(8,128)(2,1)S(1)}, s32[]{:T(128)}) while((s32[]{:T(128)}, f32[32,128,512]{2,1,0:T(8,128)}, s32[5,16]{1,0:T(8,128)S(1)}, ...), condition=%wide.region_9.10_spmd, body=%wide.region_7.9_spmd.sunk | while | flops 269485152 | bytes 23597596 | solution.py:48
  252.5 3.7 fusion.71
  256.1 9.5 %scatter_fusion.1 = f32[32,128,512]{2,1,0:T(8,128)} fusion(f32[32,128,512]{2,1,0:T(8,128)} %get-tuple-element.326, s32[16]{0:T(128)S(1)} %get-tuple-element.287, f32[16,128,512]{2,1,0:T(8,128)} %fusion.71), kind=kCustom, calls=%fused_computation.4.clone.1 | custom fusion | flops 1048576 | bytes 12582976 | tf_op jit(solution)/shard_map/while/body/eval_jaxpr/scatter-add | solution.py:45
  266.4 3.7 fusion.71
  270.0 9.6 %scatter_fusion.1 = f32[32,128,512]{2,1,0:T(8,128)} fusion(f32[32,128,512]{2,1,0:T(8,128)} %get-tuple-element.326, s32[16]{0:T(128)S(1)} %get-tuple-element.287, f32[16,128,512]{2,1,0:T(8,128)} %fusion.71), kind=kCustom, calls=%fused_computation.4.clone.1 | custom fusion | flops 1048576 | bytes 12582976 | tf_op jit(solution)/shard_map/while/body/eval_jaxpr/scatter-add | solution.py:45
  280.3 3.7 fusion.71
  284.0 9.6 %scatter_fusion.1 = f32[32,128,512]{2,1,0:T(8,128)} fusion(f32[32,128,512]{2,1,0:T(8,128)} %get-tuple-element.326, s32[16]{0:T(128)S(1)} %get-tuple-element.287, f32[16,128,512]{2,1,0:T(8,128)} %fusion.71), kind=kCustom, calls=%fused_computation.4.clone.1 | custom fusion | flops 1048576 | bytes 12582976 | tf_op jit(solution)/shard_map/while/body/eval_jaxpr/scatter-add | solution.py:45
  294.4 3.7 fusion.71
  298.0 9.7 %scatter_fusion.1 = f32[32,128,512]{2,1,0:T(8,128)} fusion(f32[32,128,512]{2,1,0:T(8,128)} %get-tuple-element.326, s32[16]{0:T(128)S(1)} %get-tuple-element.287, f32[16,128,512]{2,1,0:T(8,128)} %fusion.71), kind=kCustom, calls=%fused_computation.4.clone.1 | custom fusion | flops 1048576 | bytes 12582976 | tf_op jit(solution)/shard_map/while/body/eval_jaxpr/scatter-add | solution.py:45
  308.4 3.7 fusion.71
  312.1 9.5 %scatter_fusion.1 = f32[32,128,512]{2,1,0:T(8,128)} fusion(f32[32,128,512]{2,1,0:T(8,128)} %get-tuple-element.326, s32[16]{0:T(128)S(1)} %get-tuple-element.287, f32[16,128,512]{2,1,0:T(8,128)} %fusion.71), kind=kCustom, calls=%fused_computation.4.clone.1 | custom fusion | flops 1048576 | bytes 12582976 | tf_op jit(solution)/shard_map/while/body/eval_jaxpr/scatter-add | solution.py:45
  321.6 5.9 convert_element_type.91
  327.9 74.9 %while.32 = (s32[]{:T(128)}, f32[8,128,512]{2,1,0:T(8,128)S(1)}, s32[5,16]{1,0:T(8,128)S(1)}, bf16[5,16,128,128]{2,3,1,0:T(8,128)(2,1)}, s32[5,16]{1,0:T(8,128)S(1)}, /*index=5*/bf16[32,128,512]{2,1,0:T(8,128)(2,1)}, s32[]{:T(128)}) while((s32[]{:T(128)}, f32[8,128,512]{2,1,0:T(8,128)S(1)}, s32[5,16]{1,0:T(8,128)S(1)}, ...), condition=%wide.region_13.14_spmd, body=%wide.region_11.13_spmd.sunk | while | flops 269485152 | bytes 23597596 | solution.py:69
  327.9 4.2 gather_fusion.2
  332.1 4.4 fusion.75
  336.5 6.2 scatter_fusion.2
  342.8 4.3 gather_fusion.2
  347.1 4.5 fusion.75
  351.6 6.3 scatter_fusion.2
  357.9 4.3 gather_fusion.2
  362.2 4.5 fusion.75
  366.6 6.1 scatter_fusion.2
  372.8 4.2 gather_fusion.2
  377.0 4.8 fusion.75
  381.8 6.2 scatter_fusion.2
  388.0 4.2 gather_fusion.2
  392.2 4.5 fusion.75
  396.7 6.1 scatter_fusion.2
  404.0 12.2 %reduce-scatter.6.cloned.1.call-done = bf16[128,512]{1,0:T(8,128)(2,1)} async-done(((bf16[4096,512]{1,0:T(8,128)(2,1)}), bf16[128,512]{1,0:T(8,128)(2,1)}) %reduce-scatter.6.cloned.1.call-update) | async-done | bytes 131088 | tf_op jit(solution)/shard_map/reduce_scatter | solution.py:114
  416.3 2.0 convolution_multiply_fusion
  418.2 39.2 %reduce-scatter.8.cloned.1.call-done = bf16[128,512]{1,0:T(8,128)(2,1)} async-done(((bf16[1024,512]{1,0:T(8,128)(2,1)}), bf16[128,512]{1,0:T(8,128)(2,1)}) %reduce-scatter.8.cloned.1.call-update) | async-done | bytes 131088 | tf_op jit(solution)/shard_map/reduce_scatter | solution.py:124
  457.4 2.0 convolution_multiply_fusion.1
  460.3 257.8 %all-reduce.4.cloned.1.call-done = (f32[128,512]{1,0:T(8,128)}, f32[512,128]{1,0:T(8,128)}) async-done(((f32[128,512]{1,0:T(8,128)}, f32[512,128]{1,0:T(8,128)}), (f32[128,512]{1,0:T(8,128)}, f32[512,128]{1,0:T(8,128)})) %all-reduce.4.cloned.1.call-update) | async-done | bytes 524304 | tf_op jit(solution)/shard_map/psum | solution.py:137
  (114 shorter events, 29.3 us)
Async XLA Ops:
  7.2 202.5 %copy-start = (bf16[512,128]{1,0:T(8,128)(2,1)S(1)}, bf16[512,128]{1,0:T(8,128)(2,1)}, u32[]{:S(2)}) copy-start(bf16[512,128]{1,0:T(8,128)(2,1)} %param.17) | copy-start | bytes 393220
  7.2 200.7 %reduce-scatter.4.cloned.1.call-start = ((), (), s32[]{:S(2)}) async-start(), calls=%async_computation.3 | async-start | bytes 1081344 | tf_op jit(solution)/shard_map/reduce_scatter | solution.py:105
  81.8 3.0 copy-start.15
  81.8 4.2 copy-start.14
  81.8 4.3 copy-start.5
  81.8 4.3 copy-start.2
  84.7 123.2 %copy-start.8 = (bf16[128,128]{1,0:T(8,128)(2,1)S(1)}, bf16[128,128]{1,0:T(8,128)(2,1)}, u32[]{:S(2)}) copy-start(bf16[128,128]{1,0:T(8,128)(2,1)} %param.15) | copy-start | bytes 98308
  84.7 123.2 %copy-start.12 = (bf16[128,512]{1,0:T(8,128)(2,1)S(1)}, bf16[128,512]{1,0:T(8,128)(2,1)}, u32[]{:S(2)}) copy-start(bf16[128,512]{1,0:T(8,128)(2,1)} %param.16) | copy-start | bytes 393220
  84.7 125.0 %copy-start.6 = (bf16[128,128]{1,0:T(8,128)(2,1)S(1)}, bf16[128,128]{1,0:T(8,128)(2,1)}, u32[]{:S(2)}) copy-start(bf16[128,128]{1,0:T(8,128)(2,1)} %param.23) | copy-start | bytes 98308
  84.7 162.7 %all-gather.3.cloned.1.call-start = ((), (), s32[]{:S(2)}) async-start(), calls=%async_computation.4 | async-start | bytes 1179648 | tf_op jit(solution)/shard_map/all_gather | solution.py:112
  207.9 43.9 %copy-start.10 = (f32[128]{0:T(128)}, f32[128]{0:T(128)S(1)}, u32[]{:S(2)}) copy-start(f32[128]{0:T(128)S(1)} %fusion.37) | copy-start | bytes 1540
  209.6 118.0 %all-gather.5.cloned.1.call-start = ((), (), s32[]{:S(2)}) async-start(), calls=%async_computation.6 | async-start | bytes 4325376 | tf_op jit(solution)/shard_map/all_gather | solution.py:123
  210.6 205.7 %reduce-scatter.6.cloned.1.call-start = ((), (), s32[]{:S(2)}) async-start(), calls=%async_computation.5 | async-start | bytes 4325376 | tf_op jit(solution)/shard_map/reduce_scatter | solution.py:114
  247.4 4.3 copy-start.1
  327.6 129.8 %reduce-scatter.8.cloned.1.call-start = ((), (), s32[]{:S(2)}) async-start(), calls=%async_computation.7 | async-start | bytes 1179648 | tf_op jit(solution)/shard_map/reduce_scatter | solution.py:124
  402.8 13.5 %copy-start.3 = (bf16[128,512]{1,0:T(8,128)(2,1)S(1)}, bf16[128,512]{1,0:T(8,128)(2,1)}, u32[]{:S(2)}) copy-start(bf16[128,512]{1,0:T(8,128)(2,1)} %get-tuple-element.170) | copy-start | bytes 393220
  402.8 13.4 %copy-start.7 = (bf16[128,128]{1,0:T(8,128)(2,1)S(1)}, bf16[128,128]{1,0:T(8,128)(2,1)}, u32[]{:S(2)}) copy-start(bf16[128,128]{1,0:T(8,128)(2,1)} %param.23) | copy-start | bytes 98308
  402.8 13.4 %copy-start.11 = (f32[128]{0:T(128)S(1)}, f32[128]{0:T(128)}, u32[]{:S(2)}) copy-start(f32[128]{0:T(128)} %copy-done.10) | copy-start | bytes 1540
  402.8 54.6 %copy-start.9 = (bf16[128,128]{1,0:T(8,128)(2,1)S(1)}, bf16[128,128]{1,0:T(8,128)(2,1)}, u32[]{:S(2)}) copy-start(bf16[128,128]{1,0:T(8,128)(2,1)} %param.15) | copy-start | bytes 98308
  402.8 54.5 %copy-start.13 = (bf16[128,128]{1,0:T(8,128)(2,1)S(1)}, bf16[128,128]{1,0:T(8,128)(2,1)}, u32[]{:S(2)}) copy-start(bf16[128,128]{1,0:T(8,128)(2,1)} %reduce-scatter.4.cloned.1.call-done) | copy-start | bytes 98308
  402.9 54.5 %copy-start.16 = (f32[128,512]{1,0:T(8,128)S(1)}, f32[128,512]{1,0:T(8,128)}, u32[]{:S(2)}) copy-start(f32[128,512]{1,0:T(8,128)} %get-tuple-element.171) | copy-start | bytes 786436
  404.0 314.1 %all-reduce.4.cloned.1.call-start = ((), (), s32[]{:S(2)}) async-start(), calls=%async_computation.8 | async-start | bytes 1048576 | tf_op jit(solution)/shard_map/psum | solution.py:137
  416.3 43.2 %copy-start.4 = (bf16[128,512]{1,0:T(8,128)(2,1)S(1)}, bf16[128,512]{1,0:T(8,128)(2,1)}, u32[]{:S(2)}) copy-start(bf16[128,512]{1,0:T(8,128)(2,1)} %reduce-scatter.6.cloned.1.call-done) | copy-start | bytes 393220
Sparse Core Ops, SparseCore 0:
  84.8 84.2 reduce-scatter.3
  209.7 37.6 all-gather.2
  250.0 49.1 all-gather.4
  327.7 88.5 reduce-scatter.5
  418.6 38.7 reduce-scatter.7
  463.4 254.5 all-reduce.3
where the time goes:
time: 730 us; the launch traced here: 728 us
  waiting for transfers between devices  346 us (47%)
  blocking collectives  148 us (20%)
  other arithmetic  116 us (16%)
  matrix products  55 us (8%)
  local copies, waits for them, and re-layouts  47.4 us (6%)
  between operations  15.6 us (2%)
    psum x1, waiting for transfers between devices, local(): lax.psum((first_term * node_scale, second_term * node_scale), ('row', 'co...  258 us
    unnamed x1, blocking collectives  119 us
    scatter-add x10, other arithmetic, forward_accumulate(): return (running.at[rows_here].add(contrib), None)  64.6 us
    reduce_scatter x1, waiting for transfers between devices, local(): lax.psum_scatter(backward_part(tile_values, col_index, row_index, grad_ro...  39.2 us
    all_gather x1, waiting for transfers between devices, local(): panel_hidden = lax.all_gather(hidden, 'row', axis=0, tiled=True)  36.8 us
    scatter-add x5, other arithmetic, backward_accumulate(): return (running.at[cols_here].add(contrib), None)  30.8 us
    all_gather x1, blocking collectives, local(): panel_in = lax.all_gather(features, 'row', axis=0, tiled=True)  28.8 us
    dot_general x10, matrix products, forward_accumulate(): jnp.einsum('sij,sjf->sif', values_here, source_blocks[cols_here], preferr...  25 us
  transfers between devices with their start and end apart: 6, of which 4 were waited for; matrix products, arithmetic and copies ran while one was open for 22% of the time, Pallas kernels for 0%

commit v1 on v0

--- a/solution.py
+++ b/solution.py
@@ -6,6 +6,13 @@
 
 BLOCK = 128
 gelu_coef = math.sqrt(2.0 / math.pi)
+
+
+def gather_over(x, axis, d):
+    size = lax.axis_size(axis)
+    parts = jnp.stack([x for _ in range(size)])
+    parts = lax.all_to_all(parts, axis, split_axis=0, concat_axis=0)
+    return jnp.concatenate(parts, axis=d)
 
 
 def gelu_tanh(value):
@@ -99,7 +106,7 @@
     degree_part = (
         jnp.zeros((row_groups, BLOCK), jnp.float32).at[row_index].add(row_sums).reshape(-1)
     )
-    panel_in = lax.all_gather(features, "row", axis=0, tiled=True)
+    panel_in = gather_over(features, "row", 0)
     partial_in = forward_part(tile_values, row_index, col_index, panel_in, row_groups)
     degree = lax.psum_scatter(degree_part, "col", scatter_dimension=0, tiled=True)
     summed_in = lax.psum_scatter(

time: 730 us -> 718 us (0.984)
  blocking collectives: 148 us -> 123 us
  starting transfers between devices: 0.24 us -> 8.71 us
    all_gather x1 -> x0, blocking collectives: 28.8 us -> none  [local(): panel_in = lax.all_gather(features, 'row', axis=0, tiled=True)]
    all_to_all x0 -> x1, starting transfers between devices: none -> 8.47 us  [gather_over(): parts = lax.all_to_all(parts, axis, split_axis=0, concat_axis=0)]
  transfers between devices with their start and end apart: 6 -> 7, of which waited for: 4 -> 4; matrix products, arithmetic and copies ran while one was open for 22% -> 25% of each run, Pallas kernels for 0% -> 0%
where the time goes in v1:
time: 718 us; the launch traced here: 716 us
  waiting for transfers between devices  348 us (48%)
  blocking collectives  123 us (17%)
  other arithmetic  116 us (16%)
  matrix products  55 us (8%)
  local copies, waits for them, and re-layouts  49 us (7%)
  between operations  15.6 us (2%)
  starting transfers between devices  8.71 us (1%)
    psum x1, waiting for transfers between devices, local(): lax.psum((first_term * node_scale, second_term * node_scale), ('row', 'co...  258 us
    unnamed x1, blocking collectives  123 us
    scatter-add x10, other arithmetic, forward_accumulate(): return (running.at[rows_here].add(contrib), None)  64.7 us
    reduce_scatter x1, waiting for transfers between devices, local(): lax.psum_scatter(backward_part(tile_values, col_index, row_index, grad_ro...  39.1 us
    all_gather x1, waiting for transfers between devices, local(): panel_hidden = lax.all_gather(hidden, 'row', axis=0, tiled=True)  38.9 us
    scatter-add x5, other arithmetic, backward_accumulate(): return (running.at[cols_here].add(contrib), None)  30.8 us
    dot_general x10, matrix products, forward_accumulate(): jnp.einsum('sij,sjf->sif', values_here, source_blocks[cols_here], preferr...  25 us
    dot_general x5, matrix products, backward_accumulate(): jnp.einsum('sij,sif->sjf', values_here, source_blocks[rows_here], preferr...  22.6 us
  transfers between devices with their start and end apart: 7, of which 4 were waited for; matrix products, arithmetic and copies ran while one was open for 25% of the time, Pallas kernels for 0%

profile of v1, /device:TPU:2, one launch (start us, length us, event | category | flops | bytes accessed | tf_op | source)
XLA Modules:
  0.0 715.6 jit_solution(15841755999399568132)
XLA Ops:
  8.7 8.5 %all-to-all-start = ((bf16[8,128,128]{2,1,0:T(8,128)(2,1)}), bf16[8,128,128]{2,1,0:T(8,128)(2,1)S(1)}, u32[]{:S(2)}, u32[]{:S(2)}) async-start(bf16[8,128,128]{2,1,0:T(8,128)(2,1)} %stack.2), calls=%async_computation | async-start | bytes 524288 | tf_op jit(solution)/shard_map/all_to_all | solution.py:14
  22.0 4.4 copy.15
  26.4 4.0 multiply_multiply_fusion
  30.4 4.4 copy.16
  36.3 26.8 %while.30 = (s32[]{:T(128)}, f32[32,128,128]{2,1,0:T(8,128)}, s32[5,16]{1,0:T(8,128)S(1)}, bf16[5,16,128,128]{3,2,1,0:T(8,128)(2,1)}, s32[5,16]{1,0:T(8,128)S(1)}, /*index=5*/bf16[8,128,128]{2,1,0:T(8,128)(2,1)S(1)}, s32[]{:T(128)}) while((s32[]{:T(128)}, f32[32,128,128]{2,1,0:T(8,128)}, s32[5,16]{1,0:T(8,128)S(1)}, ...), condition=%wide.region_5.6_spmd, body=%wide.region_3.0_spmd.sunk | while | flops 67372128 | bytes 6296093 | solution.py:55
  38.3 3.3 scatter_fusion
  43.7 3.4 scatter_fusion
  49.1 3.3 scatter_fusion
  54.4 3.3 scatter_fusion
  59.8 3.3 scatter_fusion
  63.1 2.9 convert_element_type.85
  67.4 1.8 convert_reduce_fusion
  70.1 123.0 %all-reduce = f32[4096]{0:T(1024)S(1)} all-reduce(f32[4096]{0:T(1024)S(1)} %bitcast.120), channel_id=2, replica_groups=mesh['row'=8,'col'=32] {'col'}, use_global_device_ids=true, to_apply=%region_2.3.clone | all-reduce | flops 4096 | bytes 32768
  195.9 38.9 %all-gather.3.cloned.1.call-done = bf16[1024,512]{1,0:T(8,128)(2,1)} async-done(((bf16[128,512]{1,0:T(8,128)(2,1)}), bf16[1024,512]{1,0:T(8,128)(2,1)}) %all-gather.3.cloned.1.call-update) | async-done | bytes 1048592 | tf_op jit(solution)/shard_map/all_gather | solution.py:119
  234.9 4.3 broadcast_in_dim.12
  239.2 69.8 %while.31 = (s32[]{:T(128)}, f32[32,128,512]{2,1,0:T(8,128)}, s32[5,16]{1,0:T(8,128)S(1)}, bf16[5,16,128,128]{3,2,1,0:T(8,128)(2,1)}, s32[5,16]{1,0:T(8,128)S(1)}, /*index=5*/bf16[8,128,512]{2,1,0:T(8,128)(2,1)S(1)}, s32[]{:T(128)}) while((s32[]{:T(128)}, f32[32,128,512]{2,1,0:T(8,128)}, s32[5,16]{1,0:T(8,128)S(1)}, ...), condition=%wide.region_9.10_spmd, body=%wide.region_7.9_spmd.sunk | while | flops 269485152 | bytes 23597596 | solution.py:55
  239.9 3.7 fusion.71
  243.5 9.5 %scatter_fusion.1 = f32[32,128,512]{2,1,0:T(8,128)} fusion(f32[32,128,512]{2,1,0:T(8,128)} %get-tuple-element.326, s32[16]{0:T(128)S(1)} %get-tuple-element.287, f32[16,128,512]{2,1,0:T(8,128)} %fusion.71), kind=kCustom, calls=%fused_computation.4.clone.1 | custom fusion | flops 1048576 | bytes 12582976 | tf_op jit(solution)/shard_map/while/body/eval_jaxpr/scatter-add | solution.py:52
  253.8 3.7 fusion.71
  257.4 9.6 %scatter_fusion.1 = f32[32,128,512]{2,1,0:T(8,128)} fusion(f32[32,128,512]{2,1,0:T(8,128)} %get-tuple-element.326, s32[16]{0:T(128)S(1)} %get-tuple-element.287, f32[16,128,512]{2,1,0:T(8,128)} %fusion.71), kind=kCustom, calls=%fused_computation.4.clone.1 | custom fusion | flops 1048576 | bytes 12582976 | tf_op jit(solution)/shard_map/while/body/eval_jaxpr/scatter-add | solution.py:52
  267.7 3.7 fusion.71
  271.4 9.7 %scatter_fusion.1 = f32[32,128,512]{2,1,0:T(8,128)} fusion(f32[32,128,512]{2,1,0:T(8,128)} %get-tuple-element.326, s32[16]{0:T(128)S(1)} %get-tuple-element.287, f32[16,128,512]{2,1,0:T(8,128)} %fusion.71), kind=kCustom, calls=%fused_computation.4.clone.1 | custom fusion | flops 1048576 | bytes 12582976 | tf_op jit(solution)/shard_map/while/body/eval_jaxpr/scatter-add | solution.py:52
  281.8 3.7 fusion.71
  285.4 9.7 %scatter_fusion.1 = f32[32,128,512]{2,1,0:T(8,128)} fusion(f32[32,128,512]{2,1,0:T(8,128)} %get-tuple-element.326, s32[16]{0:T(128)S(1)} %get-tuple-element.287, f32[16,128,512]{2,1,0:T(8,128)} %fusion.71), kind=kCustom, calls=%fused_computation.4.clone.1 | custom fusion | flops 1048576 | bytes 12582976 | tf_op jit(solution)/shard_map/while/body/eval_jaxpr/scatter-add | solution.py:52
  295.8 3.7 fusion.71
  299.5 9.5 %scatter_fusion.1 = f32[32,128,512]{2,1,0:T(8,128)} fusion(f32[32,128,512]{2,1,0:T(8,128)} %get-tuple-element.326, s32[16]{0:T(128)S(1)} %get-tuple-element.287, f32[16,128,512]{2,1,0:T(8,128)} %fusion.71), kind=kCustom, calls=%fused_computation.4.clone.1 | custom fusion | flops 1048576 | bytes 12582976 | tf_op jit(solution)/shard_map/while/body/eval_jaxpr/scatter-add | solution.py:52
  309.0 5.9 convert_element_type.91
  315.3 75.0 %while.32 = (s32[]{:T(128)}, f32[8,128,512]{2,1,0:T(8,128)S(1)}, s32[5,16]{1,0:T(8,128)S(1)}, bf16[5,16,128,128]{2,3,1,0:T(8,128)(2,1)}, s32[5,16]{1,0:T(8,128)S(1)}, /*index=5*/bf16[32,128,512]{2,1,0:T(8,128)(2,1)}, s32[]{:T(128)}) while((s32[]{:T(128)}, f32[8,128,512]{2,1,0:T(8,128)S(1)}, s32[5,16]{1,0:T(8,128)S(1)}, ...), condition=%wide.region_13.14_spmd, body=%wide.region_11.13_spmd.sunk | while | flops 269485152 | bytes 23597596 | solution.py:76
  315.3 4.2 gather_fusion.2
  319.5 4.4 fusion.75
  323.9 6.2 scatter_fusion.2
  330.2 4.3 gather_fusion.2
  334.5 4.5 fusion.75
  339.0 6.2 scatter_fusion.2
  345.3 4.3 gather_fusion.2
  349.6 4.5 fusion.75
  354.1 6.1 scatter_fusion.2
  360.2 4.2 gather_fusion.2
  364.4 4.8 fusion.75
  369.2 6.2 scatter_fusion.2
  375.4 4.3 gather_fusion.2
  379.7 4.5 fusion.75
  384.1 6.1 scatter_fusion.2
  391.5 12.2 %reduce-scatter.6.cloned.1.call-done = bf16[128,512]{1,0:T(8,128)(2,1)} async-done(((bf16[4096,512]{1,0:T(8,128)(2,1)}), bf16[128,512]{1,0:T(8,128)(2,1)}) %reduce-scatter.6.cloned.1.call-update) | async-done | bytes 131088 | tf_op jit(solution)/shard_map/reduce_scatter | solution.py:121
  403.7 2.0 convolution_multiply_fusion
  405.6 39.1 %reduce-scatter.8.cloned.1.call-done = bf16[128,512]{1,0:T(8,128)(2,1)} async-done(((bf16[1024,512]{1,0:T(8,128)(2,1)}), bf16[128,512]{1,0:T(8,128)(2,1)}) %reduce-scatter.8.cloned.1.call-update) | async-done | bytes 131088 | tf_op jit(solution)/shard_map/reduce_scatter | solution.py:131
  444.7 2.0 convolution_multiply_fusion.1
  447.6 257.8 %all-reduce.4.cloned.1.call-done = (f32[128,512]{1,0:T(8,128)}, f32[512,128]{1,0:T(8,128)}) async-done(((f32[128,512]{1,0:T(8,128)}, f32[512,128]{1,0:T(8,128)}), (f32[128,512]{1,0:T(8,128)}, f32[512,128]{1,0:T(8,128)})) %all-reduce.4.cloned.1.call-update) | async-done | bytes 524304 | tf_op jit(solution)/shard_map/psum | solution.py:144
  (116 shorter events, 30.8 us)
Async XLA Ops:
  7.2 187.8 %copy-start = (bf16[512,128]{1,0:T(8,128)(2,1)S(1)}, bf16[512,128]{1,0:T(8,128)(2,1)}, u32[]{:S(2)}) copy-start(bf16[512,128]{1,0:T(8,128)(2,1)} %param.17) | copy-start | bytes 393220
  8.7 26.0 %all-to-all-start = ((bf16[8,128,128]{2,1,0:T(8,128)(2,1)}), bf16[8,128,128]{2,1,0:T(8,128)(2,1)S(1)}, u32[]{:S(2)}, u32[]{:S(2)}) async-start(bf16[8,128,128]{2,1,0:T(8,128)(2,1)} %stack.2), calls=%async_computation | async-start | bytes 524288 | tf_op jit(solution)/shard_map/all_to_all | solution.py:14
  17.2 176.0 %reduce-scatter.4.cloned.1.call-start = ((), (), s32[]{:S(2)}) async-start(), calls=%async_computation.4 | async-start | bytes 1081344 | tf_op jit(solution)/shard_map/reduce_scatter | solution.py:112
  63.1 3.0 copy-start.15
  63.1 4.3 copy-start.14
  63.1 4.3 copy-start.5
  63.1 4.3 copy-start.2
  66.0 127.2 %copy-start.8 = (bf16[128,128]{1,0:T(8,128)(2,1)S(1)}, bf16[128,128]{1,0:T(8,128)(2,1)}, u32[]{:S(2)}) copy-start(bf16[128,128]{1,0:T(8,128)(2,1)} %param.15) | copy-start | bytes 98308
  66.0 127.2 %copy-start.12 = (bf16[128,512]{1,0:T(8,128)(2,1)S(1)}, bf16[128,512]{1,0:T(8,128)(2,1)}, u32[]{:S(2)}) copy-start(bf16[128,512]{1,0:T(8,128)(2,1)} %param.16) | copy-start | bytes 393220
  66.0 129.0 %copy-start.6 = (bf16[128,128]{1,0:T(8,128)(2,1)S(1)}, bf16[128,128]{1,0:T(8,128)(2,1)}, u32[]{:S(2)}) copy-start(bf16[128,128]{1,0:T(8,128)(2,1)} %param.23) | copy-start | bytes 98308
  66.0 168.8 %all-gather.3.cloned.1.call-start = ((), (), s32[]{:S(2)}) async-start(), calls=%async_computation.5 | async-start | bytes 1179648 | tf_op jit(solution)/shard_map/all_gather | solution.py:119
  193.2 46.0 %copy-start.10 = (f32[128]{0:T(128)}, f32[128]{0:T(128)S(1)}, u32[]{:S(2)}) copy-start(f32[128]{0:T(128)S(1)} %fusion.37) | copy-start | bytes 1540
  195.0 120.1 %all-gather.5.cloned.1.call-start = ((), (), s32[]{:S(2)}) async-start(), calls=%async_computation.7 | async-start | bytes 4325376 | tf_op jit(solution)/shard_map/all_gather | solution.py:130
  195.9 207.8 %reduce-scatter.6.cloned.1.call-start = ((), (), s32[]{:S(2)}) async-start(), calls=%async_computation.6 | async-start | bytes 4325376 | tf_op jit(solution)/shard_map/reduce_scatter | solution.py:121
  234.9 4.3 copy-start.1
  314.9 129.8 %reduce-scatter.8.cloned.1.call-start = ((), (), s32[]{:S(2)}) async-start(), calls=%async_computation.8 | async-start | bytes 1179648 | tf_op jit(solution)/shard_map/reduce_scatter | solution.py:131
  390.3 13.4 %copy-start.3 = (bf16[128,512]{1,0:T(8,128)(2,1)S(1)}, bf16[128,512]{1,0:T(8,128)(2,1)}, u32[]{:S(2)}) copy-start(bf16[128,512]{1,0:T(8,128)(2,1)} %get-tuple-element.170) | copy-start | bytes 393220
  390.3 13.4 %copy-start.7 = (bf16[128,128]{1,0:T(8,128)(2,1)S(1)}, bf16[128,128]{1,0:T(8,128)(2,1)}, u32[]{:S(2)}) copy-start(bf16[128,128]{1,0:T(8,128)(2,1)} %param.23) | copy-start | bytes 98308
  390.3 13.4 %copy-start.11 = (f32[128]{0:T(128)S(1)}, f32[128]{0:T(128)}, u32[]{:S(2)}) copy-start(f32[128]{0:T(128)} %copy-done.10) | copy-start | bytes 1540
  390.3 54.4 %copy-start.9 = (bf16[128,128]{1,0:T(8,128)(2,1)S(1)}, bf16[128,128]{1,0:T(8,128)(2,1)}, u32[]{:S(2)}) copy-start(bf16[128,128]{1,0:T(8,128)(2,1)} %param.15) | copy-start | bytes 98308
  390.3 54.4 %copy-start.13 = (bf16[128,128]{1,0:T(8,128)(2,1)S(1)}, bf16[128,128]{1,0:T(8,128)(2,1)}, u32[]{:S(2)}) copy-start(bf16[128,128]{1,0:T(8,128)(2,1)} %reduce-scatter.4.cloned.1.call-done) | copy-start | bytes 98308
  390.3 54.4 %copy-start.16 = (f32[128,512]{1,0:T(8,128)S(1)}, f32[128,512]{1,0:T(8,128)}, u32[]{:S(2)}) copy-start(f32[128,512]{1,0:T(8,128)} %get-tuple-element.171) | copy-start | bytes 786436
  391.5 314.0 %all-reduce.4.cloned.1.call-start = ((), (), s32[]{:S(2)}) async-start(), calls=%async_computation.9 | async-start | bytes 1048576 | tf_op jit(solution)/shard_map/psum | solution.py:144
  403.7 43.1 %copy-start.4 = (bf16[128,512]{1,0:T(8,128)(2,1)S(1)}, bf16[128,512]{1,0:T(8,128)(2,1)}, u32[]{:S(2)}) copy-start(bf16[128,512]{1,0:T(8,128)(2,1)} %reduce-scatter.6.cloned.1.call-done) | copy-start | bytes 393220
Sparse Core Ops, SparseCore 0:
  66.2 86.6 reduce-scatter.3
  195.1 39.7 all-gather.2
  237.4 49.1 all-gather.4
  315.1 88.5 reduce-scatter.5
  406.0 38.6 reduce-scatter.7
  450.8 254.6 all-reduce.3
